TPU v7x, 256 devices: a whole 4x4x8 slice. The times are simulated.
256 devices in a mesh: pb: 8 (over y, core), kv: 32 (over z, x).
Axes of the slice: x: 4, y: 4, z: 8, core: 2. Of those that a mesh axis runs over, the one named last changes fastest.
Arguments:
- queries: bfloat16 [65536, 4096], P(('pb', 'kv')), may hold values from -6 to 6
- keys: bfloat16 [8192, 4096], P(('pb', 'kv')), may hold values from -6 to 6
- values: bfloat16 [8192, 4096], P(('pb', 'kv')), may hold values from -6 to 6
- key_lists: int32 [512, 8], P('pb'), may hold values from 0 to 63, as said below
- counts: int32 [512], P('pb'), may hold values from 1 to 8, as said below
Outputs:
- attended: bfloat16 [65536, 4096], P(('pb', 'kv'))
Inputs may be any that keep to these rules, and one draw needn't show every extreme that they name: For every query block the first counts entries of its row of key_lists name different key blocks; entries past counts are valid block numbers that do not take part. `counts`: some query block uses all 8 entries of its list.
All inputs are finite; a program needn't handle non-finite values.
Results may differ from a plain program's by a relative error of at most 0.011.
Values may be sent and summed in bfloat16 or wider, within the bound.
No kernel may reach another device: no remote copies, remote signals or barrier semaphores. Data moves between devices by JAX's collectives and lax.ppermute only.
A program may use at most 64 MiB of HBM per device.

v0:
```python
import math
import jax
import jax.numpy as jnp
from jax import lax
from jax.sharding import PartitionSpec as P

HEADS = 32
HD = 128
BLK = 128
MOST = 8


def regroup(split_array, kv_count, pb_count):
    tokens_each = split_array.shape[0] // (kv_count * pb_count)
    shaped = split_array.reshape(kv_count, pb_count, tokens_each, split_array.shape[1])
    return shaped.transpose(1, 0, 2, 3).reshape(-1, split_array.shape[1])


def per_device(queries, keys, values, key_lists, counts):
    kv_count = lax.axis_size("kv")
    pb_count = lax.axis_size("pb")
    head_local = HEADS // kv_count
    scaling = HD ** (-0.5)
    key_whole, value_whole = (
        lax.all_gather(keys, "pb", axis=0, tiled=True),
        lax.all_gather(values, "pb", axis=0, tiled=True),
    )
    key_split, value_split = (
        lax.all_to_all(key_whole, "kv", split_axis=1, concat_axis=0, tiled=True),
        lax.all_to_all(value_whole, "kv", split_axis=1, concat_axis=0, tiled=True),
    )
    key_heads = regroup(key_split, kv_count, pb_count)
    value_heads = regroup(value_split, kv_count, pb_count)
    key_blocks = key_heads.reshape(-1, BLK, head_local, HD)
    value_blocks = value_heads.reshape(-1, BLK, head_local, HD)
    slot_of_key = jnp.arange(MOST * BLK, dtype=jnp.int32) // BLK

    def padded_group(item):
        group_queries, group_lists, group_counts = item
        members = group_queries.shape[0]
        listed_keys = key_blocks[group_lists].reshape(members, MOST * BLK, head_local, HD)
        listed_values = value_blocks[group_lists].reshape(members, MOST * BLK, head_local, HD)
        scores = (
            jnp.einsum(
                "gqhd,gkhd->ghqk", group_queries, listed_keys, preferred_element_type=jnp.float32
            )
            * scaling
        )
        usable = (slot_of_key[None, :] < group_counts[:, None])[:, None, None, :]
        largest = jnp.max(jnp.where(usable, scores, -jnp.inf), axis=-1, keepdims=True)
        raised = jnp.where(usable, jnp.exp(scores - largest), 0.0)
        totals = jnp.sum(raised, axis=-1, keepdims=True)
        weights = (raised / totals).astype(jnp.bfloat16)
        output = jnp.einsum(
            "ghqk,gkhd->gqhd", weights, listed_values, preferred_element_type=jnp.float32
        )
        return output.astype(jnp.bfloat16)

    query_blocks = queries.reshape(-1, BLK, queries.shape[1])
    exchanged = lax.all_to_all(query_blocks, "kv", split_axis=2, concat_axis=0, tiled=True)
    block_total = exchanged.shape[0]
    rows = exchanged.shape[1]
    per_group = math.gcd(block_total, max(1, 512 // rows))
    group_total = block_total // per_group
    grouped = exchanged.reshape(group_total, per_group, rows, head_local, HD)
    lists_grouped = key_lists.reshape(group_total, per_group, key_lists.shape[1])
    counts_grouped = counts.reshape(group_total, per_group)
    produced = lax.map(padded_group, (grouped, lists_grouped, counts_grouped))
    joined = produced.reshape(block_total, rows, head_local * HD)
    result = lax.all_to_all(joined, "kv", split_axis=0, concat_axis=2, tiled=True)
    return result.reshape(queries.shape)


def solution(mesh):
    return jax.shard_map(
        per_device,
        mesh=mesh,
        in_specs=(
            P(("pb", "kv"), None),
            P(("pb", "kv"), None),
            P(("pb", "kv"), None),
            P("pb", None),
            P("pb"),
        ),
        out_specs=P(("pb", "kv"), None),
        check_vma=False,
    )
```

profile of v0, /device:TPU:2, one launch (start us, length us, event | category | flops | bytes accessed | tf_op | source)
XLA Modules:
  0.0 411.0 jit_solution(12888155072686574849)
XLA Ops:
  6.5 6.2 %copy.31 = bf16[2,128,4096]{1,0,2:T(2,128)(2,1)} copy(bf16[2,128,4096]{2,1,0:T(8,128)(2,1)} %bitcast.84) | data formatting | bytes 4194304 | tf_op jit(solution)/shard_map/reshape | solution.py:59
  12.7 11.6 %all-to-all-start.1 = ((bf16[2,128,4096]{1,0,2:T(2,128)(2,1)}), bf16[2,128,4096]{1,0,2:T(2,128)(2,1)S(1)}, u32[]{:S(2)}, u32[]{:S(2)}) async-start(bf16[2,128,4096]{1,0,2:T(2,128)(2,1)} %copy.31), calls=%async_computation.1 | async-start | bytes 4194304 | tf_op jit(solution)/shard_map/all_to_all | solution.py:60
  25.1 30.8 %all-gather.5.cloned.1.call-done = bf16[256,4096]{1,0:T(8,128)(2,1)} async-done(((bf16[32,4096]{1,0:T(8,128)(2,1)}), bf16[256,4096]{1,0:T(8,128)(2,1)}) %all-gather.5.cloned.1.call-update) | async-done | bytes 2097168 | tf_op jit(solution)/shard_map/all_gather | solution.py:25
  55.9 4.1 copy.34
  60.0 13.6 %all-to-all-done.1 = bf16[2,128,4096]{1,0,2:T(2,128)(2,1)S(1)} async-done(((bf16[2,128,4096]{1,0,2:T(2,128)(2,1)}), bf16[2,128,4096]{1,0,2:T(2,128)(2,1)S(1)}, u32[]{:S(2)}, u32[]{:S(2)}) %all-to-all-start.1) | async-done | bytes 2097184 | tf_op jit(solution)/shard_map/all_to_all | solution.py:60
  73.6 6.9 %all-to-all-start.2 = ((bf16[256,32,128]{0,2,1:T(8,128)(2,1)}), bf16[256,32,128]{0,2,1:T(8,128)(2,1)}, u32[]{:S(2)}, u32[]{:S(2)}) async-start(bf16[256,32,128]{0,2,1:T(8,128)(2,1)} %bitcast.76), calls=%async_computation.2 | async-start | bytes 4194304 | tf_op jit(solution)/shard_map/all_to_all | solution.py:29
  81.2 30.8 %all-gather.3.cloned.1.call-done = bf16[256,4096]{1,0:T(8,128)(2,1)} async-done(((bf16[32,4096]{1,0:T(8,128)(2,1)}), bf16[256,4096]{1,0:T(8,128)(2,1)}) %all-gather.3.cloned.1.call-update) | async-done | bytes 2097168 | tf_op jit(solution)/shard_map/all_gather | solution.py:26
  112.1 4.1 copy.28
  116.1 12.9 %all-to-all-done.2 = bf16[256,32,128]{0,2,1:T(8,128)(2,1)} async-done(((bf16[256,32,128]{0,2,1:T(8,128)(2,1)}), bf16[256,32,128]{0,2,1:T(8,128)(2,1)}, u32[]{:S(2)}, u32[]{:S(2)}) %all-to-all-start.2) | async-done | bytes 2097184 | tf_op jit(solution)/shard_map/all_to_all | solution.py:29
  129.1 6.7 %all-to-all-start = ((bf16[256,32,128]{0,2,1:T(8,128)(2,1)}), bf16[256,32,128]{0,2,1:T(8,128)(2,1)}, u32[]{:S(2)}, u32[]{:S(2)}) async-start(bf16[256,32,128]{0,2,1:T(8,128)(2,1)} %bitcast.77), calls=%async_computation | async-start | bytes 4194304 | tf_op jit(solution)/shard_map/all_to_all | solution.py:30
  137.7 4.1 copy.33
  141.7 4.1 copy.35
  145.8 2.0 copy.36
  147.8 37.0 %all-to-all-done = bf16[256,32,128]{0,2,1:T(8,128)(2,1)} async-done(((bf16[256,32,128]{0,2,1:T(8,128)(2,1)}), bf16[256,32,128]{0,2,1:T(8,128)(2,1)}, u32[]{:S(2)}, u32[]{:S(2)}) %all-to-all-start) | async-done | bytes 2097184 | tf_op jit(solution)/shard_map/all_to_all | solution.py:30
  184.8 4.1 copy.29
  188.9 3.4 copy.30
  192.2 154.8 %while.11 = (s32[]{:T(128)}, bf16[16,4,128,1,128]{4,2,1,0,3:T(8,128)(2,1)}, s32[16,4,8]{2,1,0:T(4,128)S(1)}, bf16[64,128,1,128]{3,1,0,2:T(8,128)(2,1)}, s32[16,4...) while((s32[]{:T(128)}, ...), condition=%wide.region_3.4_spmd.clone, body=%wide.region_0.3_spmd.clone.sunk | while | flops 272709728 | bytes 15493133 | solution.py:68
  194.5 2.0 fusion.36
  196.5 2.3 gather_fusion
  198.9 2.2 fusion.37
  204.2 2.0 fusion.36
  206.2 2.3 gather_fusion
  208.6 2.2 fusion.37
  213.9 2.0 fusion.36
  215.9 2.3 gather_fusion
  218.2 2.2 fusion.37
  223.5 2.0 fusion.36
  225.6 2.3 gather_fusion
  227.9 2.2 fusion.37
  233.2 2.0 fusion.36
  235.2 2.3 gather_fusion
  237.6 2.2 fusion.37
  242.9 2.0 fusion.36
  244.9 2.3 gather_fusion
  247.3 2.2 fusion.37
  252.6 2.0 fusion.36
  254.6 2.3 gather_fusion
  256.9 2.2 fusion.37
  262.2 2.0 fusion.36
  264.3 2.3 gather_fusion
  266.6 2.2 fusion.37
  271.9 2.0 fusion.36
  273.9 2.3 gather_fusion
  276.3 2.2 fusion.37
  281.6 2.0 fusion.36
  283.6 2.3 gather_fusion
  285.9 2.2 fusion.37
  291.3 2.0 fusion.36
  293.3 2.3 gather_fusion
  295.6 2.2 fusion.37
  300.9 2.0 fusion.36
  302.9 2.3 gather_fusion
  305.3 2.2 fusion.37
  310.6 2.0 fusion.36
  312.6 2.3 gather_fusion
  315.0 2.2 fusion.37
  322.3 2.3 gather_fusion
  324.6 2.2 fusion.37
  332.0 2.3 gather_fusion
  334.3 2.2 fusion.37
  341.6 2.3 gather_fusion
  344.0 2.2 fusion.37
  347.0 53.5 %all_to_all.62 = bf16[64,128,128]{2,1,0:T(8,128)(2,1)S(1)} all-to-all(bf16[64,128,128]{2,1,0:T(8,128)(2,1)} %bitcast.85), channel_id=1, replica_groups=mesh['pb'=8,'kv'=32] {'kv'}, dimensions={0} | all-to-all | bytes 4194304 | tf_op jit(solution)/shard_map/all_to_all | solution.py:70
  401.8 2.3 copy.45
  (176 shorter events, 60.0 us)
Async XLA Ops:
  12.7 60.9 %all-to-all-start.1 = ((bf16[2,128,4096]{1,0,2:T(2,128)(2,1)}), bf16[2,128,4096]{1,0,2:T(2,128)(2,1)S(1)}, u32[]{:S(2)}, u32[]{:S(2)}) async-start(bf16[2,128,4096]{1,0,2:T(2,128)(2,1)} %copy.31), calls=%async_computation.1 | async-start | bytes 4194304 | tf_op jit(solution)/shard_map/all_to_all | solution.py:60
  24.3 31.6 %all-gather.5.cloned.1.call-start = ((), (), s32[]{:S(2)}) async-start(), calls=%async_computation.5 | async-start | bytes 2359296 | tf_op jit(solution)/shard_map/all_gather | solution.py:25
  73.6 55.5 %all-to-all-start.2 = ((bf16[256,32,128]{0,2,1:T(8,128)(2,1)}), bf16[256,32,128]{0,2,1:T(8,128)(2,1)}, u32[]{:S(2)}, u32[]{:S(2)}) async-start(bf16[256,32,128]{0,2,1:T(8,128)(2,1)} %bitcast.76), calls=%async_computation.2 | async-start | bytes 4194304 | tf_op jit(solution)/shard_map/all_to_all | solution.py:29
  80.5 31.6 %all-gather.3.cloned.1.call-start = ((), (), s32[]{:S(2)}) async-start(), calls=%async_computation.4 | async-start | bytes 2359296 | tf_op jit(solution)/shard_map/all_gather | solution.py:26
  129.1 6.8 %copy-start = (s32[64,8]{0,1:T(8,128)S(1)}, s32[64,8]{0,1:T(8,128)}, u32[]{:S(2)}) copy-start(s32[64,8]{0,1:T(8,128)} %param.10) | copy-start | bytes 6148
  129.1 6.9 %copy-start.1 = (s32[64]{0:T(128)S(1)}, s32[64]{0:T(128)}, u32[]{:S(2)}) copy-start(s32[64]{0:T(128)} %param.11) | copy-start | bytes 772
  129.1 55.7 %all-to-all-start = ((bf16[256,32,128]{0,2,1:T(8,128)(2,1)}), bf16[256,32,128]{0,2,1:T(8,128)(2,1)}, u32[]{:S(2)}, u32[]{:S(2)}) async-start(bf16[256,32,128]{0,2,1:T(8,128)(2,1)} %bitcast.77), calls=%async_computation | async-start | bytes 4194304 | tf_op jit(solution)/shard_map/all_to_all | solution.py:30
Sparse Core Ops, SparseCore 0:
  27.0 28.8 all-gather.4
  83.2 28.8 all-gather.2
where the time goes:
time: 413 us; the launch traced here: 411 us
  waiting for transfers between devices  127 us (31%)
  local copies, waits for them, and re-layouts  101 us (24%)
  matrix products  56.6 us (14%)
  blocking collectives  53.5 us (13%)
  other arithmetic  33.6 us (8%)
  starting transfers between devices  25.4 us (6%)
  between operations  13.5 us (3%)
    all_to_all x1, blocking collectives, per_device(): lax.all_to_all(joined, 'kv', split_axis=0, concat_axis=2, tiled=True)  53.5 us
    gather x16, local copies, waits for them, and re-layouts, padded_group(): value_blocks[group_lists].reshape(members, MOST * BLK, head_local, HD)  37.4 us
    all_to_all x1, waiting for transfers between devices, per_device(): lax.all_to_all(value_whole, 'kv', split_axis=1, concat_axis=0, tiled=True)  37 us
    dot_general x16, matrix products, padded_group(): jnp.einsum('ghqk,gkhd->gqhd', weights, listed_values, preferred_element_t...  35.1 us
    sub x16, other arithmetic, padded_group(): raised = jnp.where(usable, jnp.exp(scores - largest), 0.0)  32.1 us
    all_gather x1, waiting for transfers between devices, per_device(): lax.all_gather(keys, 'pb', axis=0, tiled=True)  30.8 us
    all_gather x1, waiting for transfers between devices, per_device(): lax.all_gather(values, 'pb', axis=0, tiled=True)  30.8 us
    dot_general x16, matrix products, padded_group(): jnp.einsum('gqhd,gkhd->ghqk', group_queries, listed_keys, preferred_eleme...  21.5 us
  transfers between devices with their start and end apart: 5, of which 5 were waited for; matrix products, arithmetic and copies ran while one was open for 5% of the time, Pallas kernels for 0%

commit v1 on v0

--- a/solution.py
+++ b/solution.py
@@ -21,10 +21,20 @@
     pb_count = lax.axis_size("pb")
     head_local = HEADS // kv_count
     scaling = HD ** (-0.5)
-    key_whole, value_whole = (
-        lax.all_gather(keys, "pb", axis=0, tiled=True),
-        lax.all_gather(values, "pb", axis=0, tiled=True),
-    )
+
+    def _detail_space(z_in):
+        ready = jnp.concatenate(
+            lax.all_to_all(
+                jnp.stack([z_in] * lax.axis_size("pb"), axis=0),
+                axis_name="pb",
+                split_axis=0,
+                concat_axis=0,
+            ),
+            axis=0,
+        )
+        return ready
+
+    key_whole, value_whole = (lax.all_gather(keys, "pb", axis=0, tiled=True), _detail_space(values))
     key_split, value_split = (
         lax.all_to_all(key_whole, "kv", split_axis=1, concat_axis=0, tiled=True),
         lax.all_to_all(value_whole, "kv", split_axis=1, concat_axis=0, tiled=True),

time: 413 us -> 441 us (1.068)
  waiting for transfers between devices: 127 us -> 151 us
    all_to_all x1, waiting for transfers between devices: 13.6 us -> 44.9 us  [per_device(): lax.all_to_all(query_blocks, 'kv', split_axis=2, concat_axis=0, tiled=True)]
    all_gather x1 -> x0, waiting for transfers between devices: 30.8 us -> none  [per_device(): lax.all_gather(values, 'pb', axis=0, tiled=True)]
    all_to_all x1, waiting for transfers between devices: 12.9 us -> 39.6 us  [per_device(): lax.all_to_all(key_whole, 'kv', split_axis=1, concat_axis=0, tiled=True)]
    gather x16, local copies, waits for them, and re-layouts: 12 us -> 37.4 us  [padded_group(): key_blocks[group_lists].reshape(members, MOST * BLK, head_local, HD)]
    gather x16, local copies, waits for them, and re-layouts: 37.4 us -> 11.9 us  [padded_group(): value_blocks[group_lists].reshape(members, MOST * BLK, head_local, HD)]
    all_to_all x1, waiting for transfers between devices: 37 us -> 15.6 us  [per_device(): lax.all_to_all(value_whole, 'kv', split_axis=1, concat_axis=0, tiled=True)]
    all_to_all x0 -> x1, waiting for transfers between devices: none -> 21 us  [_detail_space(): lax.all_to_all(jnp.stack([z_in] * lax.axis_size('pb'), axis=0), axis_name...]
    all_to_all x0 -> x1, starting transfers between devices: none -> 4.47 us  [_detail_space(): lax.all_to_all(jnp.stack([z_in] * lax.axis_size('pb'), axis=0), axis_name...]
where the time goes in v1:
time: 441 us; the launch traced here: 439 us
  waiting for transfers between devices  151 us (34%)
  local copies, waits for them, and re-layouts  101 us (23%)
  matrix products  56.6 us (13%)
  blocking collectives  54 us (12%)
  other arithmetic  33.7 us (8%)
  starting transfers between devices  28.8 us (7%)
  between operations  13.5 us (3%)
    all_to_all x1, blocking collectives, per_device(): lax.all_to_all(joined, 'kv', split_axis=0, concat_axis=2, tiled=True)  54 us
    all_to_all x1, waiting for transfers between devices, per_device(): lax.all_to_all(query_blocks, 'kv', split_axis=2, concat_axis=0, tiled=True)  44.9 us
    all_to_all x1, waiting for transfers between devices, per_device(): lax.all_to_all(key_whole, 'kv', split_axis=1, concat_axis=0, tiled=True)  39.6 us
    gather x16, local copies, waits for them, and re-layouts, padded_group(): key_blocks[group_lists].reshape(members, MOST * BLK, head_local, HD)  37.4 us
    dot_general x16, matrix products, padded_group(): jnp.einsum('ghqk,gkhd->gqhd', weights, listed_values, preferred_element_t...  35.1 us
    sub x16, other arithmetic, padded_group(): raised = jnp.where(usable, jnp.exp(scores - largest), 0.0)  32.2 us
    all_gather x1, waiting for transfers between devices, per_device(): lax.all_gather(keys, 'pb', axis=0, tiled=True)  28.8 us
    dot_general x16, matrix products, padded_group(): jnp.einsum('gqhd,gkhd->ghqk', group_queries, listed_keys, preferred_eleme...  21.4 us
  transfers between devices with their start and end apart: 5, of which 5 were waited for; matrix products, arithmetic and copies ran while one was open for 5% of the time, Pallas kernels for 0%

profile of v1, /device:TPU:2, one launch (start us, length us, event | category | flops | bytes accessed | tf_op | source)
XLA Modules:
  0.0 439.1 jit_solution(14084261264104227928)
XLA Ops:
  6.5 2.5 stack.2
  9.0 4.5 %all-to-all-start = ((bf16[8,32,4096]{2,1,0:T(8,128)(2,1)}), bf16[8,32,4096]{2,1,0:T(8,128)(2,1)S(1)}, u32[]{:S(2)}, u32[]{:S(2)}) async-start(bf16[8,32,4096]{2,1,0:T(8,128)(2,1)} %stack.2), calls=%async_computation | async-start | bytes 4194304 | tf_op jit(solution)/shard_map/all_to_all | solution.py:27
  13.5 6.2 %copy.29 = bf16[2,128,4096]{1,0,2:T(2,128)(2,1)} copy(bf16[2,128,4096]{2,1,0:T(8,128)(2,1)} %bitcast.87) | data formatting | bytes 4194304 | tf_op jit(solution)/shard_map/reshape | solution.py:69
  19.7 21.0 %all-to-all-done = bf16[8,32,4096]{2,1,0:T(8,128)(2,1)S(1)} async-done(((bf16[8,32,4096]{2,1,0:T(8,128)(2,1)}), bf16[8,32,4096]{2,1,0:T(8,128)(2,1)S(1)}, u32[]{:S(2)}, u32[]{:S(2)}) %all-to-all-start) | async-done | bytes 2097184 | tf_op jit(solution)/shard_map/all_to_all | solution.py:27
  42.0 11.6 %all-to-all-start.2 = ((bf16[2,128,4096]{1,0,2:T(2,128)(2,1)}), bf16[2,128,4096]{1,0,2:T(2,128)(2,1)S(1)}, u32[]{:S(2)}, u32[]{:S(2)}) async-start(bf16[2,128,4096]{1,0,2:T(2,128)(2,1)} %copy.29), calls=%async_computation.2 | async-start | bytes 4194304 | tf_op jit(solution)/shard_map/all_to_all | solution.py:70
  53.7 2.1 copy.41
  55.7 2.1 copy.27
  57.9 44.9 %all-to-all-done.2 = bf16[2,128,4096]{1,0,2:T(2,128)(2,1)S(1)} async-done(((bf16[2,128,4096]{1,0,2:T(2,128)(2,1)}), bf16[2,128,4096]{1,0,2:T(2,128)(2,1)S(1)}, u32[]{:S(2)}, u32[]{:S(2)}) %all-to-all-start.2) | async-done | bytes 2097184 | tf_op jit(solution)/shard_map/all_to_all | solution.py:70
  102.7 6.9 %all-to-all-start.1 = ((bf16[256,32,128]{2,0,1:T(8,128)(2,1)}), bf16[256,32,128]{2,0,1:T(8,128)(2,1)}, u32[]{:S(2)}, u32[]{:S(2)}) async-start(bf16[256,32,128]{2,0,1:T(8,128)(2,1)} %copy.27), calls=%async_computation.1 | async-start | bytes 4194304 | tf_op jit(solution)/shard_map/all_to_all | solution.py:40
  110.4 28.8 %all-gather.2.cloned.1.call-done = bf16[256,4096]{1,0:T(8,128)(2,1)} async-done(((bf16[32,4096]{1,0:T(8,128)(2,1)}), bf16[256,4096]{1,0:T(8,128)(2,1)}) %all-gather.2.cloned.1.call-update) | async-done | bytes 2097168 | tf_op jit(solution)/shard_map/all_gather | solution.py:37
  139.2 4.1 copy.32
  143.3 15.6 %all-to-all-done.1 = bf16[256,32,128]{2,0,1:T(8,128)(2,1)} async-done(((bf16[256,32,128]{2,0,1:T(8,128)(2,1)}), bf16[256,32,128]{2,0,1:T(8,128)(2,1)}, u32[]{:S(2)}, u32[]{:S(2)}) %all-to-all-start.1) | async-done | bytes 2097184 | tf_op jit(solution)/shard_map/all_to_all | solution.py:40
  158.9 5.8 %all-to-all-start.3 = ((bf16[256,32,128]{0,2,1:T(8,128)(2,1)}), bf16[256,32,128]{0,2,1:T(8,128)(2,1)}, u32[]{:S(2)}, u32[]{:S(2)}) async-start(bf16[256,32,128]{0,2,1:T(8,128)(2,1)} %bitcast.79), calls=%async_computation.3 | async-start | bytes 4194304 | tf_op jit(solution)/shard_map/all_to_all | solution.py:39
  166.5 4.1 copy.31
  170.6 2.0 copy.28
  172.6 39.6 %all-to-all-done.3 = bf16[256,32,128]{0,2,1:T(8,128)(2,1)} async-done(((bf16[256,32,128]{0,2,1:T(8,128)(2,1)}), bf16[256,32,128]{0,2,1:T(8,128)(2,1)}, u32[]{:S(2)}, u32[]{:S(2)}) %all-to-all-start.3) | async-done | bytes 2097184 | tf_op jit(solution)/shard_map/all_to_all | solution.py:39
  212.2 4.1 copy.33
  216.4 3.4 copy.34
  219.7 154.8 %while.11 = (s32[]{:T(128)}, bf16[16,4,128,1,128]{4,2,1,0,3:T(8,128)(2,1)}, s32[16,4,8]{2,1,0:T(4,128)S(1)}, bf16[64,128,1,128]{3,1,0,2:T(8,128)(2,1)S(1)}, s32[...) while((s32[]{:T(128)}, ...), condition=%wide.region_3.4_spmd.clone, body=%wide.region_0.3_spmd.clone.sunk | while | flops 272709728 | bytes 15493133 | solution.py:78
  219.8 2.3 gather_fusion.1
  223.6 2.0 fusion.36
  226.4 2.2 fusion.37
  229.5 2.3 gather_fusion.1
  233.3 2.0 fusion.36
  236.1 2.2 fusion.37
  239.2 2.3 gather_fusion.1
  243.0 2.0 fusion.36
  245.8 2.2 fusion.37
  248.9 2.3 gather_fusion.1
  252.7 2.0 fusion.36
  255.4 2.2 fusion.37
  258.5 2.3 gather_fusion.1
  262.3 2.0 fusion.36
  265.1 2.2 fusion.37
  268.2 2.3 gather_fusion.1
  272.0 2.0 fusion.36
  274.8 2.2 fusion.37
  277.9 2.3 gather_fusion.1
  281.7 2.0 fusion.36
  284.5 2.2 fusion.37
  287.6 2.3 gather_fusion.1
  291.4 2.0 fusion.36
  294.1 2.2 fusion.37
  297.2 2.3 gather_fusion.1
  301.0 2.0 fusion.36
  303.8 2.2 fusion.37
  306.9 2.3 gather_fusion.1
  310.7 2.0 fusion.36
  313.5 2.2 fusion.37
  316.6 2.3 gather_fusion.1
  323.2 2.2 fusion.37
  326.3 2.3 gather_fusion.1
  330.1 2.0 fusion.36
  332.8 2.2 fusion.37
  336.0 2.3 gather_fusion.1
  342.5 2.2 fusion.37
  345.6 2.3 gather_fusion.1
  352.2 2.2 fusion.37
  355.3 2.3 gather_fusion.1
  361.9 2.2 fusion.37
  365.0 2.3 gather_fusion.1
  371.5 2.2 fusion.37
  374.6 54.0 %all_to_all.67 = bf16[64,128,128]{2,1,0:T(8,128)(2,1)S(1)} all-to-all(bf16[64,128,128]{2,1,0:T(8,128)(2,1)} %bitcast.88), channel_id=1, replica_groups=mesh['pb'=8,'kv'=32] {'kv'}, dimensions={0} | all-to-all | bytes 4194304 | tf_op jit(solution)/shard_map/all_to_all | solution.py:80
  430.0 2.3 copy.44
  (178 shorter events, 64.5 us)
Async XLA Ops:
  9.0 31.7 %all-to-all-start = ((bf16[8,32,4096]{2,1,0:T(8,128)(2,1)}), bf16[8,32,4096]{2,1,0:T(8,128)(2,1)S(1)}, u32[]{:S(2)}, u32[]{:S(2)}) async-start(bf16[8,32,4096]{2,1,0:T(8,128)(2,1)} %stack.2), calls=%async_computation | async-start | bytes 4194304 | tf_op jit(solution)/shard_map/all_to_all | solution.py:27
  40.7 1.3 copy-start
  42.0 60.7 %all-to-all-start.2 = ((bf16[2,128,4096]{1,0,2:T(2,128)(2,1)}), bf16[2,128,4096]{1,0,2:T(2,128)(2,1)S(1)}, u32[]{:S(2)}, u32[]{:S(2)}) async-start(bf16[2,128,4096]{1,0,2:T(2,128)(2,1)} %copy.29), calls=%async_computation.2 | async-start | bytes 4194304 | tf_op jit(solution)/shard_map/all_to_all | solution.py:70
  102.7 56.2 %all-to-all-start.1 = ((bf16[256,32,128]{2,0,1:T(8,128)(2,1)}), bf16[256,32,128]{2,0,1:T(8,128)(2,1)}, u32[]{:S(2)}, u32[]{:S(2)}) async-start(bf16[256,32,128]{2,0,1:T(8,128)(2,1)} %copy.27), calls=%async_computation.1 | async-start | bytes 4194304 | tf_op jit(solution)/shard_map/all_to_all | solution.py:40
  109.6 29.6 %all-gather.2.cloned.1.call-start = ((), (), s32[]{:S(2)}) async-start(), calls=%async_computation.5 | async-start | bytes 2359296 | tf_op jit(solution)/shard_map/all_gather | solution.py:37
  158.9 5.8 %copy-start.1 = (s32[64,8]{0,1:T(8,128)S(1)}, s32[64,8]{0,1:T(8,128)}, u32[]{:S(2)}) copy-start(s32[64,8]{0,1:T(8,128)} %param.10) | copy-start | bytes 6148
  158.9 5.9 %copy-start.2 = (s32[64]{0:T(128)S(1)}, s32[64]{0:T(128)}, u32[]{:S(2)}) copy-start(s32[64]{0:T(128)} %param.11) | copy-start | bytes 772
  158.9 53.3 %all-to-all-start.3 = ((bf16[256,32,128]{0,2,1:T(8,128)(2,1)}), bf16[256,32,128]{0,2,1:T(8,128)(2,1)}, u32[]{:S(2)}, u32[]{:S(2)}) async-start(bf16[256,32,128]{0,2,1:T(8,128)(2,1)} %bitcast.79), calls=%async_computation.3 | async-start | bytes 4194304 | tf_op jit(solution)/shard_map/all_to_all | solution.py:39
Sparse Core Ops, SparseCore 0:
  112.3 26.8 all-gather.1
